TPU v7x, 32 devices: a whole 2x2x4 slice. The times are simulated.
32 devices in a mesh: grp: 8 (over z, x), rep: 4 (over y, core).
Axes of the slice: x: 2, y: 2, z: 4, core: 2. Of those that a mesh axis runs over, the one named last changes fastest.
Arguments:
- three_center: bfloat16 [4, 64, 32, 6, 4096], P('rep', 'grp'), may hold values from -2 to 2
- metric: bfloat16 [4, 64, 64], P('rep'), may hold values from -0.75 to 0.75
- occupied: bfloat16 [2048, 48], replicated, may hold values from -0.3125 to 0.3125
- nu_list: int32 [32, 6], replicated, may hold values from 0 to 31, as said below
- nu_count: int32 [32], replicated, may hold values from 1 to 6
- block_size: int32 [32], replicated, may hold values from 32 to 64
Outputs:
- exchange_matrix: float32 [2048, 2048], P('rep', 'grp')
Inputs may be any that keep to these rules, and one draw needn't show every extreme that they name: `nu_list`: entry 0 of row m is m itself; the other entries of a row are distinct blocks other than m.
All inputs are finite; a program needn't handle non-finite values.
Results may differ from a plain program's by a relative error of at most 0.0024.
Values may be sent and summed in bfloat16 or wider, within the bound.
No kernel may reach another device: no remote copies, remote signals or barrier semaphores. Data moves between devices by JAX's collectives and lax.ppermute only.
A program may use at most 192 MiB of HBM per device.

v0:
```python
import jax
import jax.numpy as jnp
from jax import lax
from jax.sharding import PartitionSpec as P

NB = 64


def body(three_center, metric, occupied, nu_list, nu_count, block_size):
    n_mu, knu = nu_list.shape
    n_occ = occupied.shape[1]
    aux_dev = three_center.shape[1]
    lanes = jnp.arange(NB, dtype=jnp.int32)
    row_live = lanes[None, :] < block_size[:, None]
    col_live = lanes[None, None, :] < block_size[nu_list][:, :, None]
    slot_live = jnp.arange(knu, dtype=jnp.int32)[None, :] < nu_count[:, None]
    mask = row_live[:, None, :, None] & col_live[:, :, None, :] & slot_live[:, :, None, None]
    blocks = three_center[0].reshape(aux_dev, n_mu, knu, NB, NB)
    masked = jnp.where(mask[None], blocks, jnp.zeros((), jnp.bfloat16))
    picked = occupied.reshape(n_mu, NB, n_occ)[nu_list]
    half = jnp.einsum(
        "qmkab,mkbi->qmai", masked, picked, preferred_element_type=jnp.float32
    ).astype(jnp.bfloat16)
    half = half.reshape(aux_dev, n_mu, NB * n_occ)
    regrouped = lax.all_to_all(half, "grp", split_axis=1, concat_axis=0, tiled=True)
    n_aux = regrouped.shape[0]
    mu_dev = regrouped.shape[1]
    regrouped = regrouped.reshape(n_aux, mu_dev, NB, n_occ)
    orbital = jnp.einsum(
        "pq,qmai->mapi", metric[0], regrouped, preferred_element_type=jnp.float32
    ).astype(jnp.bfloat16)
    orbital = orbital.reshape(mu_dev * NB, n_aux * n_occ)
    term = jnp.dot(
        lax.all_gather(orbital, "grp", axis=0, tiled=True),
        orbital.T,
        preferred_element_type=jnp.float32,
    )
    return lax.psum_scatter(term, "rep", scatter_dimension=0, tiled=True)


def solution(mesh):
    return jax.shard_map(
        body,
        mesh=mesh,
        in_specs=(P("rep", "grp", None, None, None), P("rep", None, None), P(), P(), P(), P()),
        out_specs=P("rep", "grp"),
        check_vma=False,
    )
```

profile of v0, /device:TPU:0, one launch (start us, length us, event | category | flops | bytes accessed | tf_op | source)
XLA Modules:
  0.0 370.5 jit_solution(7674496762199158850)
XLA Ops:
  6.5 0.7 compare_select_fusion
  7.3 0.7 iota_compare_fusion.1
  8.0 0.7 iota_compare_fusion.2
  8.8 0.1 reshape.66
  8.9 1.6 gather_fusion.1
  10.6 0.1 iota_compare_fusion
  10.7 0.4 reshape.60
  11.1 0.2 copy.23
  11.3 1.0 gather_fusion
  12.3 34.4 %reshape_squeeze.3 = bf16[8,32,6,64,64]{4,3,1,2,0:T(8,128)(2,1)} reshape(bf16[1,8,32,6,4096]{4,2,3,1,0:T(8,128)(2,1)} %param.6) | data formatting | bytes 25165824 | tf_op jit(solution)/shard_map/reshape;squeeze | solution.py:18
  46.7 2.3 and_and_fusion
  49.0 17.0 %fusion.3 = bf16[8,32,64,48]{2,3,0,1:T(8,128)(2,1)} fusion(bf16[32,6,64,48,1]{2,3,1,4,0:T(8,128)(2,1)S(1)} %bitcast.47, bf16[8,32,6,64,64]{4,3,1,2,0:T(8,128)(2,1)} %reshape_squeeze.3, pred[32,6,64,64]{3,2,1,0:T(8,128)(4,1)} %and_and_fusion), kind=kOutput, calls=%fused_computation.8 | convolution fusion | flops 611057664 | bytes 16121856 | tf_op jit(solution)/shard_map/qmkab,mkbi->qmai/dot_general | solution.py:21
  66.0 6.2 %copy.33 = bf16[8,32,64,48]{3,2,0,1:T(8,128)(2,1)} copy(bf16[8,32,64,48]{2,3,0,1:T(8,128)(2,1)} %fusion.3) | data formatting | bytes 3145728 | tf_op jit(solution)/shard_map/reshape | solution.py:24
  72.2 8.0 %reshape.87 = bf16[8,32,3072]{2,0,1:T(8,128)(2,1)S(1)} reshape(bf16[8,32,64,48]{3,2,0,1:T(8,128)(2,1)} %copy.33) | data formatting | bytes 3145728 | tf_op jit(solution)/shard_map/reshape | solution.py:24
  80.2 44.1 %all_to_all.15 = bf16[8,32,3072]{2,0,1:T(8,128)(2,1)S(1)} all-to-all(bf16[8,32,3072]{2,0,1:T(8,128)(2,1)S(1)} %reshape.87), channel_id=1, replica_groups=mesh['grp'=8,'rep'=4] {'grp'}, dimensions={1} | all-to-all | bytes 3145728 | tf_op jit(solution)/shard_map/all_to_all | solution.py:25
  124.2 0.1 copy.40
  124.3 5.3 %reshape.62 = bf16[64,4,64,48]{3,2,0,1:T(8,128)(2,1)} reshape(bf16[8,8,4,3072]{3,1,0,2:T(8,128)(2,1)S(1)} %bitcast.46) | data formatting | bytes 3145728 | tf_op jit(solution)/shard_map/reshape | solution.py:28
  129.7 6.4 %copy.28 = bf16[64,4,64,48]{0,2,3,1:T(8,128)(2,1)S(1)} copy(bf16[64,4,64,48]{3,2,0,1:T(8,128)(2,1)} %reshape.62) | data formatting | bytes 3145728 | tf_op jit(solution)/shard_map/reshape | solution.py:28
  136.1 2.6 convert_bitcast_fusion
  138.7 6.3 %copy.29 = bf16[4,64,64,48]{1,0,3,2:T(4,128)(2,1)S(1)} copy(bf16[4,64,64,48]{2,1,3,0:T(8,128)(2,1)} %convert_bitcast_fusion) | data formatting | bytes 3145728 | tf_op jit(solution)/shard_map/convert_element_type | solution.py:31
  145.1 3.0 reshape.63
  148.2 175.7 %all-gather.2.cloned.1.call-done = bf16[2048,3072]{0,1:T(8,128)(2,1)} async-done(((bf16[256,3072]{0,1:T(8,128)(2,1)}), bf16[2048,3072]{0,1:T(8,128)(2,1)}) %all-gather.2.cloned.1.call-update) | async-done | bytes 12582928 | tf_op jit(solution)/shard_map/all_gather | solution.py:34
  323.9 10.0 %fusion.6 = f32[2048,256]{1,0:T(8,128)} fusion(bf16[2048,3072]{0,1:T(8,128)(2,1)} %all-gather.2.cloned.1.call-done, bf16[256,3072]{0,1:T(8,128)(2,1)} %reshape.63), kind=kOutput, calls=%fused_computation.18 | convolution fusion | flops 3221225472 | bytes 16252928 | tf_op jit(solution)/shard_map/dot_general | solution.py:33
  333.9 29.8 %reduce-scatter.2.cloned.1.call-done = f32[512,256]{1,0:T(8,128)} async-done(((f32[2048,256]{1,0:T(8,128)}), f32[512,256]{1,0:T(8,128)}) %reduce-scatter.2.cloned.1.call-update) | async-done | bytes 524304 | tf_op jit(solution)/shard_map/reduce_scatter | solution.py:38
  (13 shorter events, 0.3 us)
Async XLA Ops:
  6.5 129.6 %copy-start = (bf16[1,64,64]{2,1,0:T(8,128)(2,1)S(1)}, bf16[1,64,64]{2,1,0:T(8,128)(2,1)}, u32[]{:S(2)}) copy-start(bf16[1,64,64]{2,1,0:T(8,128)(2,1)} %param.7) | copy-start | bytes 24580
  6.5 2.4 copy-start.1
  6.5 317.3 %all-gather.2.cloned.1.call-start = ((), (), s32[]{:S(2)}) async-start(), calls=%async_computation.2 | async-start | bytes 14155776 | tf_op jit(solution)/shard_map/all_gather | solution.py:34
  8.9 1.8 copy-start.2
  148.1 215.5 %reduce-scatter.2.cloned.1.call-start = ((), (), s32[]{:S(2)}) async-start(), calls=%async_computation.3 | async-start | bytes 2621440 | tf_op jit(solution)/shard_map/reduce_scatter | solution.py:38
Sparse Core Ops, SparseCore 0:
  148.2 175.5 all-gather.1
  334.0 29.5 reduce-scatter.1
where the time goes:
time: 372 us; the launch traced here: 370 us
  waiting for transfers between devices  205 us (55%)
  local copies, waits for them, and re-layouts  73.1 us (20%)
  blocking collectives  44.1 us (12%)
  matrix products  29.6 us (8%)
  between operations  13.5 us (4%)
  other arithmetic  4.59 us (1%)
    all_gather x1, waiting for transfers between devices, body(): lax.all_gather(orbital, 'grp', axis=0, tiled=True)  176 us
    all_to_all x1, blocking collectives, body(): lax.all_to_all(half, 'grp', split_axis=1, concat_axis=0, tiled=True)  44.1 us
    another operation x1, local copies, waits for them, and re-layouts, body(): blocks = three_center[0].reshape(aux_dev, n_mu, knu, NB, NB)  34.4 us
    reduce_scatter x1, waiting for transfers between devices, body(): return lax.psum_scatter(term, 'rep', scatter_dimension=0, tiled=True)  29.8 us
    dot_general x1, matrix products, body(): jnp.einsum('qmkab,mkbi->qmai', masked, picked, preferred_element_type=jnp...  17 us
    reshape x2, local copies, waits for them, and re-layouts, body(): half = half.reshape(aux_dev, n_mu, NB * n_occ)  14.1 us
    reshape x2, local copies, waits for them, and re-layouts, body(): regrouped = regrouped.reshape(n_aux, mu_dev, NB, n_occ)  11.8 us
    dot_general x1, matrix products, body(): jnp.dot(lax.all_gather(orbital, 'grp', axis=0, tiled=True), orbital.T, pr...  9.99 us
  transfers between devices with their start and end apart: 2, of which 2 were waited for; matrix products, arithmetic and copies ran while one was open for 0% of the time, Pallas kernels for 0%

commit v1 on v0

--- a/solution.py
+++ b/solution.py
@@ -4,6 +4,18 @@
 from jax.sharding import PartitionSpec as P
 
 NB = 64
+
+
+def doubled_up(shard, axis, dim):
+    ways, here, hop = (lax.axis_size(axis), lax.axis_index(axis), shard.shape[dim])
+    line, have = (shard, 1)
+    while have < ways:
+        line = jnp.concatenate(
+            [line, lax.ppermute(line, axis, [(d, (d - have) % ways) for d in range(ways)])],
+            axis=dim,
+        )
+        have = 2 * have
+    return jnp.roll(line, here * hop, axis=dim)
 
 
 def body(three_center, metric, occupied, nu_list, nu_count, block_size):
@@ -30,11 +42,7 @@
         "pq,qmai->mapi", metric[0], regrouped, preferred_element_type=jnp.float32
     ).astype(jnp.bfloat16)
     orbital = orbital.reshape(mu_dev * NB, n_aux * n_occ)
-    term = jnp.dot(
-        lax.all_gather(orbital, "grp", axis=0, tiled=True),
-        orbital.T,
-        preferred_element_type=jnp.float32,
-    )
+    term = jnp.dot(doubled_up(orbital, "grp", 0), orbital.T, preferred_element_type=jnp.float32)
     return lax.psum_scatter(term, "rep", scatter_dimension=0, tiled=True)
 
 

time: 372 us -> 597 us (1.60)
  waiting for transfers between devices: 205 us -> 400 us
  local copies, waits for them, and re-layouts: 73.1 us -> 98.4 us
    ppermute x0 -> x3, waiting for transfers between devices: none -> 367 us  [doubled_up(): lax.ppermute(line, axis, [(d, (d - have) % ways) for d in range(ways)])]
    all_gather x1 -> x0, waiting for transfers between devices: 176 us -> none  [body(): lax.all_gather(orbital, 'grp', axis=0, tiled=True)]
    unnamed x6 -> x17, local copies, waits for them, and re-layouts: 0.01 us -> 15.4 us
    concatenate x0 -> x1, local copies, waits for them, and re-layouts: none -> 6.15 us  [doubled_up(): return jnp.roll(line, here * hop, axis=dim)]
  transfers between devices with their start and end apart: 2 -> 4, of which waited for: 2 -> 4; matrix products, arithmetic and copies ran while one was open for 0% -> 1% of each run, Pallas kernels for 0% -> 0%
where the time goes in v1:
time: 597 us; the launch traced here: 596 us
  waiting for transfers between devices  400 us (67%)
  local copies, waits for them, and re-layouts  98.4 us (16%)
  blocking collectives  44.1 us (7%)
  matrix products  27.6 us (5%)
  between operations  13.5 us (2%)
  other arithmetic  7.76 us (1%)
    ppermute x3, waiting for transfers between devices, doubled_up(): lax.ppermute(line, axis, [(d, (d - have) % ways) for d in range(ways)])  367 us
    all_to_all x1, blocking collectives, body(): lax.all_to_all(half, 'grp', split_axis=1, concat_axis=0, tiled=True)  44.1 us
    another operation x1, local copies, waits for them, and re-layouts, body(): blocks = three_center[0].reshape(aux_dev, n_mu, knu, NB, NB)  34.4 us
    reduce_scatter x1, waiting for transfers between devices, body(): return lax.psum_scatter(term, 'rep', scatter_dimension=0, tiled=True)  33.5 us
    dot_general x1, matrix products, body(): jnp.einsum('qmkab,mkbi->qmai', masked, picked, preferred_element_type=jnp...  17 us
    unnamed x17, local copies, waits for them, and re-layouts  15.4 us
    reshape x2, local copies, waits for them, and re-layouts, body(): half = half.reshape(aux_dev, n_mu, NB * n_occ)  14.1 us
  transfers between devices with their start and end apart: 4, of which 4 were waited for; matrix products, arithmetic and copies ran while one was open for 1% of the time, Pallas kernels for 0%

profile of v1, /device:TPU:0, one launch (start us, length us, event | category | flops | bytes accessed | tf_op | source)
XLA Modules:
  0.0 595.6 jit_solution(8123244254941862198)
XLA Ops:
  9.7 1.6 gather_fusion.1
  12.6 34.4 %reshape_squeeze.3 = bf16[8,32,6,64,64]{4,3,1,2,0:T(8,128)(2,1)} reshape(bf16[1,8,32,6,4096]{4,2,3,1,0:T(8,128)(2,1)} %param.6) | data formatting | bytes 25165824 | tf_op jit(solution)/shard_map/reshape;squeeze | solution.py:30
  47.0 2.3 and_and_fusion
  49.3 17.0 %fusion.5 = bf16[8,32,64,48]{2,3,0,1:T(8,128)(2,1)} fusion(bf16[32,6,64,48,1]{2,3,1,4,0:T(8,128)(2,1)S(1)} %bitcast.46, bf16[8,32,6,64,64]{4,3,1,2,0:T(8,128)(2,1)} %reshape_squeeze.3, pred[32,6,64,64]{3,2,1,0:T(8,128)(4,1)} %and_and_fusion), kind=kOutput, calls=%fused_computation.11 | convolution fusion | flops 611057664 | bytes 16121856 | tf_op jit(solution)/shard_map/qmkab,mkbi->qmai/dot_general | solution.py:33
  66.3 6.2 %copy.33 = bf16[8,32,64,48]{3,2,0,1:T(8,128)(2,1)} copy(bf16[8,32,64,48]{2,3,0,1:T(8,128)(2,1)} %fusion.5) | data formatting | bytes 3145728 | tf_op jit(solution)/shard_map/reshape | solution.py:36
  72.5 8.0 %reshape.87 = bf16[8,32,3072]{2,0,1:T(8,128)(2,1)S(1)} reshape(bf16[8,32,64,48]{3,2,0,1:T(8,128)(2,1)} %copy.33) | data formatting | bytes 3145728 | tf_op jit(solution)/shard_map/reshape | solution.py:36
  80.5 44.1 %all_to_all.15 = bf16[8,32,3072]{2,0,1:T(8,128)(2,1)S(1)} all-to-all(bf16[8,32,3072]{2,0,1:T(8,128)(2,1)S(1)} %reshape.87), channel_id=1, replica_groups=mesh['grp'=8,'rep'=4] {'grp'}, dimensions={1} | all-to-all | bytes 3145728 | tf_op jit(solution)/shard_map/all_to_all | solution.py:37
  124.6 5.3 reshape.62
  130.0 6.4 %copy.28 = bf16[64,4,64,48]{0,2,3,1:T(8,128)(2,1)S(1)} copy(bf16[64,4,64,48]{3,2,0,1:T(8,128)(2,1)} %reshape.62) | data formatting | bytes 3145728 | tf_op jit(solution)/shard_map/reshape | solution.py:40
  136.4 2.6 convert_bitcast_fusion
  139.0 7.3 %copy.29 = bf16[4,64,64,48]{1,0,3,2:T(4,128)(2,1)} copy(bf16[4,64,64,48]{2,1,3,0:T(8,128)(2,1)} %convert_bitcast_fusion) | data formatting | bytes 3145728 | tf_op jit(solution)/shard_map/convert_element_type | solution.py:43
  146.3 4.8 reshape.63
  151.1 2.4 collective-permute-start
  153.5 33.3 %collective-permute-done = bf16[256,3072]{0,1:T(8,128)(2,1)S(1)} collective-permute-done((bf16[256,3072]{0,1:T(8,128)(2,1)S(1)}, bf16[256,3072]{0,1:T(8,128)(2,1)S(1)}, u32[]{:S(2)}, u32[]{:S(2)}) %collective-permute-start) | collective-permute-done | bytes 1572896 | tf_op jit(solution)/shard_map/ppermute | solution.py:14
  187.0 1.4 collective-permute-start.1
  188.4 67.3 %collective-permute-done.1 = bf16[512,3072]{0,1:T(8,128)(2,1)S(1)} collective-permute-done((bf16[512,3072]{0,1:T(8,128)(2,1)S(1)}, bf16[512,3072]{0,1:T(8,128)(2,1)S(1)}, u32[]{:S(2)}, u32[]{:S(2)}) %collective-permute-start.1) | collective-permute-done | bytes 3145760 | tf_op jit(solution)/shard_map/ppermute | solution.py:14
  255.7 3.6 pad_maximum_fusion
  262.3 1.9 constant_dynamic-update-slice_fusion.5
  264.2 266.1 %collective-permute-done.2 = bf16[1024,3072]{0,1:T(8,128)(2,1)} collective-permute-done((bf16[1024,3072]{0,1:T(8,128)(2,1)}, bf16[1024,3072]{0,1:T(8,128)(2,1)}, u32[]{:S(2)}, u32[]{:S(2)}) %collective-permute-start.2) | collective-permute-done | bytes 6291488 | tf_op jit(solution)/shard_map/ppermute | solution.py:14
  530.3 6.1 %constant_dynamic-update-slice_fusion.4 = bf16[4096,3072]{0,1:T(8,128)(2,1)} fusion(bf16[4096,3072]{0,1:T(8,128)(2,1)} %constant_dynamic-update-slice_fusion.5, bf16[1024,3072]{0,1:T(8,128)(2,1)} %collective-permute-done.2), kind=kLoop, calls=%fused_computation.20 | loop fusion | bytes 12582912
  539.1 1.9 constant_dynamic-update-slice_fusion.1
  541.1 6.2 %constant_dynamic-update-slice_fusion = bf16[4096,3072]{0,1:T(8,128)(2,1)} fusion(bf16[4096,3072]{0,1:T(8,128)(2,1)} %constant_dynamic-update-slice_fusion.1, bf16[1024,3072]{0,1:T(8,128)(2,1)} %collective-permute-done.2), kind=kLoop, calls=%fused_computation.16 | loop fusion | bytes 12582912 | tf_op jit(solution)/shard_map/jit(_roll_dynamic)/concatenate | solution.py:18
  547.2 8.0 %fusion.2 = f32[2048,256]{1,0:T(8,128)} fusion(bf16[256,3072]{0,1:T(8,128)(2,1)S(1)} %reshape.63, bf16[4096,3072]{0,1:T(8,128)(2,1)} %constant_dynamic-update-slice_fusion, s32[]{:T(128)S(6)} %select_n.24), kind=kOutput, calls=%fused_computation.5 | convolution fusion | flops 3221225472 | bytes 16252932 | tf_op jit(solution)/shard_map/dot_general | solution.py:45
  555.2 33.5 %reduce-scatter.2.cloned.1.call-done = f32[512,256]{1,0:T(8,128)} async-done(((f32[2048,256]{1,0:T(8,128)}), f32[512,256]{1,0:T(8,128)}) %reduce-scatter.2.cloned.1.call-update) | async-done | bytes 524304 | tf_op jit(solution)/shard_map/reduce_scatter | solution.py:46
  (30 shorter events, 10.5 us)
Async XLA Ops:
  6.5 129.9 %copy-start = (bf16[1,64,64]{2,1,0:T(8,128)(2,1)S(1)}, bf16[1,64,64]{2,1,0:T(8,128)(2,1)}, u32[]{:S(2)}) copy-start(bf16[1,64,64]{2,1,0:T(8,128)(2,1)} %param.7) | copy-start | bytes 24580
  6.5 3.2 copy-start.1
  6.5 582.2 %reduce-scatter.2.cloned.1.call-start = ((), (), s32[]{:S(2)}) async-start(), calls=%async_computation.2 | async-start | bytes 2621440 | tf_op jit(solution)/shard_map/reduce_scatter | solution.py:46
  11.2 1.3 copy-start.4
  151.1 35.7 %collective-permute-start = (bf16[256,3072]{0,1:T(8,128)(2,1)S(1)}, bf16[256,3072]{0,1:T(8,128)(2,1)S(1)}, u32[]{:S(2)}, u32[]{:S(2)}) collective-permute-start(bf16[256,3072]{0,1:T(8,128)(2,1)S(1)} %reshape.63), channel_id=1, source_target_pairs={{0,28},{4,0},{8,4},{12,8},{16,12},{20,16},{24,20},{28,24},{1,29},{... | collective-permute-start | bytes 4718600 | tf_op jit(solution)/shard_map/ppermute | solution.py:14
  187.0 68.6 %collective-permute-start.1 = (bf16[512,3072]{0,1:T(8,128)(2,1)S(1)}, bf16[512,3072]{0,1:T(8,128)(2,1)S(1)}, u32[]{:S(2)}, u32[]{:S(2)}) collective-permute-start(bf16[512,3072]{0,1:T(8,128)(2,1)S(1)} %pad_maximum_fusion.1), channel_id=1, source_target_pairs={{0,24},{4,28},{8,0},{12,4},{16,8},{20,12},{24,16},{28,20},{1,25},{... | collective-permute-start | bytes 9437192 | tf_op jit(solution)/shard_map/ppermute | solution.py:14
  255.7 3.6 copy-start.2
  259.3 271.1 %collective-permute-start.2 = (bf16[1024,3072]{0,1:T(8,128)(2,1)}, bf16[1024,3072]{0,1:T(8,128)(2,1)}, u32[]{:S(2)}, u32[]{:S(2)}) collective-permute-start(bf16[1024,3072]{0,1:T(8,128)(2,1)} %pad_maximum_fusion), channel_id=1, source_target_pairs={{0,16},{4,20},{8,24},{12,28},{16,0},{20,4},{24,8},{28,12},{1,17},{... | collective-permute-start | bytes 18874376 | tf_op jit(solution)/shard_map/ppermute | solution.py:14
  259.5 2.7 copy-start.3
Sparse Core Ops, SparseCore 0:
  555.3 33.3 reduce-scatter.1
